TPU v7x, 256 devices: a whole 4x4x8 slice. The times are simulated.
256 devices in a mesh: spot: 16 (over x, y_hi, core), gene: 16 (over y_lo, z).
Axes of the slice: x: 4, y: 4 (y_hi: 2, y_lo: 2; y = y_hi * 2 + y_lo), z: 8, core: 2. Of those that a mesh axis runs over, the one named last changes fastest.
Arguments:
- counts: int32 [64, 512, 4096], P('spot', None, 'gene'), may hold values from 0 to 56, as said below
- tissue: int32 [64, 512], P('spot'), may hold values from 0 to 1
- tile_ids: int32 [64, 512], P('spot'), may hold values from 0 to 32767, as said below
Outputs:
- statistic: float32 [4096, 4096], P('gene', 'spot')
Inputs may be any that keep to these rules, and one draw needn't show every extreme that they name: `counts`: whole numbers of molecules. `tile_ids`: bins of one tile form a rectangle of the grid; tiles are bands of rows crossed with bands of columns.
All inputs are finite; a program needn't handle non-finite values.
Results may differ from a plain program's by a relative error of at most 0.003.
Values may be sent and summed in bfloat16 or wider, within the bound.
No kernel may reach another device: no remote copies, remote signals or barrier semaphores. Data moves between devices by JAX's collectives and lax.ppermute only.
A program may use at most 64 MiB of HBM per device.

v0:
```python
import jax
import jax.numpy as jnp
from jax import lax
from jax.sharding import PartitionSpec as P

stencil_taps = [
    (row_off, col_off, 1.0 / (row_off * row_off + col_off * col_off))
    for row_off in range(-2, 3)
    for col_off in range(-2, 3)
    if row_off != 0 or col_off != 0
]
contract_bins = (((0,), (0,)), ((), ()))


def padded(cells, sides, width):
    for axis, dim in sides:
        count = lax.axis_size(axis)
        ends = count - 1
        head = lax.slice_in_dim(cells, 0, width, axis=dim)
        tail = lax.slice_in_dim(cells, cells.shape[dim] - width, cells.shape[dim], axis=dim)
        cells = jnp.concatenate(
            [
                lax.ppermute(tail, axis, [(i, (i + 1) % count) for i in range(ends)]),
                cells,
                lax.ppermute(head, axis, [((i + 1) % count, i) for i in range(ends)]),
            ],
            axis=dim,
        )
    return cells


def cross_panel(left, right):
    return lax.dot_general(left, right, contract_bins, preferred_element_type=jnp.float32)


def shards(counts, tissue, tile_ids):
    row_count, col_count, panel_width = counts.shape
    tile_code = tile_ids * 2 + tissue
    code_rims = padded(tile_code, (("spot", 0),), 2)
    code_wide = jnp.pad(code_rims, ((0, 0), (2, 2)))
    tissue_wide = (code_wide % 2).astype(jnp.float32)
    ids_wide = code_wide // 2
    in_tissue = tissue.astype(jnp.float32)
    weight_sq = jnp.zeros((row_count, col_count), jnp.float32)
    same_list = []
    for row_off, col_off, weight in stencil_taps:
        near_ids = ids_wide[
            2 + row_off : 2 + row_off + row_count, 2 + col_off : 2 + col_off + col_count
        ]
        near_tissue = tissue_wide[
            2 + row_off : 2 + row_off + row_count, 2 + col_off : 2 + col_off + col_count
        ]
        same_tile = (near_ids == tile_ids).astype(jnp.float32)
        weight_sq = weight_sq + weight * weight * same_tile * near_tissue
        same_list.append(same_tile)
    pair_local = jnp.sum(in_tissue * weight_sq)
    count_local = jnp.sum(in_tissue)
    values = counts.astype(jnp.float32)
    masked = values * in_tissue[:, :, None]
    first_sums = jnp.sum(masked, axis=(0, 1))
    total_first, tissue_count, pair_norm = lax.psum((first_sums, count_local, pair_local), "spot")
    gene_mean = total_first / tissue_count
    centred = (values - gene_mean) * in_tissue[:, :, None]
    variance = lax.psum(jnp.sum(centred * centred, axis=(0, 1)), "spot") / tissue_count
    zscores = (centred / jnp.sqrt(variance + 1e-05)).astype(jnp.bfloat16)
    zscore_rims = padded(zscores, (("spot", 0),), 2)
    zscore_wide = jnp.pad(zscore_rims, ((0, 0), (2, 2), (0, 0)))
    lagged_sum = jnp.zeros(values.shape, jnp.float32)
    for (row_off, col_off, weight), same_tile in zip(stencil_taps, same_list):
        near_z = zscore_wide[
            2 + row_off : 2 + row_off + row_count, 2 + col_off : 2 + col_off + col_count, :
        ]
        lagged_sum = lagged_sum + weight * same_tile[:, :, None] * near_z.astype(jnp.float32)
    lagged = lagged_sum.astype(jnp.bfloat16)
    bin_count = row_count * col_count
    flat_z = zscores.reshape(bin_count, panel_width)
    flat_lag = lagged.reshape(bin_count, panel_width)
    totals = cross_panel(flat_z, lax.all_gather(flat_lag, "gene", axis=1, tiled=True))
    share = lax.psum_scatter(totals, "spot", scatter_dimension=1, tiled=True)
    return share / jnp.sqrt(pair_norm)


def solution(mesh):
    placed = (P("spot", None, "gene"), P("spot", None), P("spot", None))
    return jax.shard_map(
        shards, mesh=mesh, in_specs=placed, out_specs=P("gene", "spot"), check_vma=False
    )
```

profile of v0, /device:TPU:32, one launch (start us, length us, event | category | flops | bytes accessed | tf_op | source)
XLA Modules:
  0.0 425.3 jit_solution(14319070710412826453)
XLA Ops:
  6.5 0.9 multiply_add_fusion
  7.4 1.7 collective-permute-start
  9.2 1.3 collective-permute-start.1
  10.5 1.3 convert_reduce_fusion
  11.8 2.0 multiply_reduce_fusion.1
  13.8 40.1 %all-reduce.3 = (f32[256]{0:T(256)S(1)}, f32[]{:T(128)}) all-reduce(f32[256]{0:T(256)S(1)} %multiply_reduce_fusion.1, f32[]{:T(128)} %convert_reduce_fusion), channel_id=1, replica_groups=mesh['spot'=16,'gene'=16] {'spot'}, use_global_device_ids=true, to_apply=%region_1.2 | all-reduce | flops 257 | bytes 2056 | tf_op jit(solution)/shard_map/psum | solution.py:61
  53.8 0.6 broadcast_divide_fusion.1
  54.5 0.4 multiply_reduce_fusion
  54.9 0.1 add_select_fusion.1
  55.2 0.2 broadcast_select_fusion.19
  55.4 0.7 fusion.14
  56.1 33.8 %all-reduce.2 = (f32[256]{0:T(256)S(1)}, f32[]{:T(128)}) all-reduce(f32[256]{0:T(256)S(1)} %multiply_reduce_fusion, f32[]{:T(128)} %fusion.14), channel_id=1, replica_groups=mesh['spot'=16,'gene'=16] {'spot'}, use_global_device_ids=true, to_apply=%region_5.6 | all-reduce | flops 257 | bytes 2056 | tf_op jit(solution)/shard_map/psum | solution.py:64
  89.9 0.7 add_sqrt_fusion
  90.6 0.4 divide_convert_fusion
  91.0 1.8 collective-permute-start.2
  92.8 1.3 collective-permute-start.3
  94.1 0.2 collective-permute-done.2
  94.3 2.3 collective-permute-done.3
  96.6 0.7 fusion.5
  97.4 12.2 %add_convert_fusion = bf16[4,512,256]{2,1,0:T(8,128)(2,1)} fusion(bf16[4,512,256]{2,1,0:T(8,128)(2,1)S(1)} %divide_convert_fusion, bf16[2,512,256]{2,1,0:T(8,128)(2,1)S(1)} %collective-permute-done.3, bf16[2,512,256]{2,1,0:T(8,128)(2,1)S(1)} %collective-permute-done.2, bf16[8,516,256]{2,1,0:T(8,128)(2,1)S(1)} %fusion.5, f32[4,512]{1,0:T(4,128)S(1)} %get-tuple-element.93, ...), kind=kLoop, calls=%fused_computation.8 | loop fusion | flops 39845888 | bytes 24313856 | tf_op jit(solution)/shard_map/convert_element_type | solution.py:74
  109.7 210.7 %all-gather.2.cloned.1.call-done = bf16[2048,4096]{1,0:T(8,128)(2,1)} async-done(((bf16[2048,256]{1,0:T(8,128)(2,1)}), bf16[2048,4096]{1,0:T(8,128)(2,1)}) %all-gather.2.cloned.1.call-update) | async-done | bytes 16777232 | tf_op jit(solution)/shard_map/all_gather | solution.py:78
  320.3 10.1 %fusion.43 = f32[256,4096]{1,0:T(8,128)} fusion(bf16[2048,256]{1,0:T(8,128)(2,1)S(1)} %bitcast.4, bf16[2048,4096]{1,0:T(8,128)(2,1)} %all-gather.2.cloned.1.call-done), kind=kOutput, calls=%fused_computation.137 | convolution fusion | flops 4294967296 | bytes 22020096 | tf_op jit(solution)/shard_map/dot_general | solution.py:33
  331.1 85.7 %reduce-scatter.2.cloned.1.call-done = f32[256,256]{1,0:T(8,128)} async-done(((f32[256,4096]{1,0:T(8,128)}), f32[256,256]{1,0:T(8,128)}) %reduce-scatter.2.cloned.1.call-update) | async-done | bytes 262160 | tf_op jit(solution)/shard_map/reduce_scatter | solution.py:79
  416.8 1.7 broadcast_divide_fusion
  (17 shorter events, 0.3 us)
Async XLA Ops:
  6.5 48.0 %copy-start = (s32[4,512,256]{2,1,0:T(8,128)S(1)}, s32[4,512,256]{2,1,0:T(8,128)}, u32[]{:S(2)}) copy-start(s32[4,512,256]{2,1,0:T(8,128)} %param.3) | copy-start | bytes 6291460
  6.5 313.8 %all-gather.2.cloned.1.call-start = ((), (), s32[]{:S(2)}) async-start(), calls=%async_computation.1 | async-start | bytes 17825792 | tf_op jit(solution)/shard_map/all_gather | solution.py:78
  7.4 47.5 %collective-permute-start = (s32[2,512]{1,0:T(2,128)S(1)}, s32[2,512]{1,0:T(2,128)S(1)}, u32[]{:S(2)}, u32[]{:S(2)}) collective-permute-start(s32[2,512]{1,0:T(2,128)S(1)} %get-tuple-element.103), channel_id=1, source_target_pairs={{0,16},{16,32},{32,48},{48,64},{64,80},{80,96},{96,112},{112,128},... | collective-permute-start | bytes 12296 | tf_op jit(solution)/shard_map/ppermute | solution.py:23
  9.2 45.7 %collective-permute-start.1 = (s32[2,512]{1,0:T(2,128)S(1)}, s32[2,512]{1,0:T(2,128)S(1)}, u32[]{:S(2)}, u32[]{:S(2)}) collective-permute-start(s32[2,512]{1,0:T(2,128)S(1)} %get-tuple-element.104), channel_id=1, source_target_pairs={{16,0},{32,16},{48,32},{64,48},{80,64},{96,80},{112,96},{128,112},... | collective-permute-start | bytes 12296 | tf_op jit(solution)/shard_map/ppermute | solution.py:25
  11.8 43.2 %copy-start.1 = (s32[4,512]{1,0:T(4,128)S(1)}, s32[4,512]{1,0:T(4,128)}, u32[]{:S(2)}) copy-start(s32[4,512]{1,0:T(4,128)} %param.5) | copy-start | bytes 24580
  11.8 43.6 %copy-start.2 = (s32[4,512]{1,0:T(4,128)S(1)}, s32[4,512]{1,0:T(4,128)}, u32[]{:S(2)}) copy-start(s32[4,512]{1,0:T(4,128)} %param.4) | copy-start | bytes 24580
  91.0 3.3 collective-permute-start.2
  92.8 3.8 collective-permute-start.3
  109.6 307.2 %reduce-scatter.2.cloned.1.call-start = ((), (), s32[]{:S(2)}) async-start(), calls=%async_computation.2 | async-start | bytes 4456448 | tf_op jit(solution)/shard_map/reduce_scatter | solution.py:79
Sparse Core Ops, SparseCore 0:
  109.8 210.5 all-gather.1
  330.6 86.1 reduce-scatter.1
where the time goes:
time: 426 us; the launch traced here: 425 us
  waiting for transfers between devices  299 us (70%)
  blocking collectives  73.8 us (17%)
  other arithmetic  22 us (5%)
  between operations  14.1 us (3%)
  matrix products  10.1 us (2%)
  starting transfers between devices  6.18 us (1%)
    all_gather x1, waiting for transfers between devices, shards(): lax.all_gather(flat_lag, 'gene', axis=1, tiled=True)  211 us
    reduce_scatter x1, waiting for transfers between devices, shards(): share = lax.psum_scatter(totals, 'spot', scatter_dimension=1, tiled=True)  85.7 us
    psum x1, blocking collectives, shards(): lax.psum((first_sums, count_local, pair_local), 'spot')  40.1 us
    psum x1, blocking collectives, shards(): lax.psum(jnp.sum(centred * centred, axis=(0, 1)), 'spot') / tissue_count  33.8 us
    convert_element_type x1, other arithmetic, shards(): lagged = lagged_sum.astype(jnp.bfloat16)  12.2 us
    dot_general x1, matrix products, cross_panel(): lax.dot_general(left, right, contract_bins, preferred_element_type=jnp.fl...  10.1 us
  transfers between devices with their start and end apart: 6, of which 4 were waited for; matrix products, arithmetic and copies ran while one was open for 1% of the time, Pallas kernels for 0%

commit v1 on v0

--- a/solution.py
+++ b/solution.py
@@ -10,6 +10,11 @@
     if row_off != 0 or col_off != 0
 ]
 contract_bins = (((0,), (0,)), ((), ()))
+
+
+def resolve_sample_here(field):
+    answer = jnp.sum(lax.all_gather(field, "spot"), axis=0)
+    return answer
 
 
 def padded(cells, sides, width):
@@ -61,7 +66,7 @@
     total_first, tissue_count, pair_norm = lax.psum((first_sums, count_local, pair_local), "spot")
     gene_mean = total_first / tissue_count
     centred = (values - gene_mean) * in_tissue[:, :, None]
-    variance = lax.psum(jnp.sum(centred * centred, axis=(0, 1)), "spot") / tissue_count
+    variance = resolve_sample_here(jnp.sum(centred * centred, axis=(0, 1))) / tissue_count
     zscores = (centred / jnp.sqrt(variance + 1e-05)).astype(jnp.bfloat16)
     zscore_rims = padded(zscores, (("spot", 0),), 2)
     zscore_wide = jnp.pad(zscore_rims, ((0, 0), (2, 2), (0, 0)))

time: 426 us -> 414 us (0.972)
  blocking collectives: 73.8 us -> 56.9 us
  waiting for transfers between devices: 299 us -> 304 us
    psum x1 -> x0, blocking collectives: 33.8 us -> none  [shards(): lax.psum(jnp.sum(centred * centred, axis=(0, 1)), 'spot') / tissue_count]
    all_gather x0 -> x1, blocking collectives: none -> 19 us  [resolve_sample_here(): answer = jnp.sum(lax.all_gather(field, 'spot'), axis=0)]
    ppermute x2, waiting for transfers between devices: 2.32 us -> 7.24 us  [padded(): lax.ppermute(head, axis, [((i + 1) % count, i) for i in range(ends)])]
  transfers between devices with their start and end apart: 6 -> 6, of which waited for: 4 -> 5; matrix products, arithmetic and copies ran while one was open for 1% -> 1% of each run, Pallas kernels for 0% -> 0%
where the time goes in v1:
time: 414 us
  waiting for transfers between devices  304 us (73%)
  blocking collectives  56.9 us (14%)
  other arithmetic  21.4 us (5%)
  between operations  14.2 us (3%)
  matrix products  10.1 us (2%)
  starting transfers between devices  6.65 us (2%)
    all_gather x1, waiting for transfers between devices, shards(): lax.all_gather(flat_lag, 'gene', axis=1, tiled=True)  211 us
    reduce_scatter x1, waiting for transfers between devices, shards(): share = lax.psum_scatter(totals, 'spot', scatter_dimension=1, tiled=True)  85.7 us
    psum x1, blocking collectives, shards(): lax.psum((first_sums, count_local, pair_local), 'spot')  37.9 us
    all_gather x1, blocking collectives, resolve_sample_here(): answer = jnp.sum(lax.all_gather(field, 'spot'), axis=0)  19 us
    convert_element_type x1, other arithmetic, shards(): lagged = lagged_sum.astype(jnp.bfloat16)  12.2 us
    dot_general x1, matrix products, cross_panel(): lax.dot_general(left, right, contract_bins, preferred_element_type=jnp.fl...  10.1 us
  transfers between devices with their start and end apart: 6, of which 5 were waited for; matrix products, arithmetic and copies ran while one was open for 1% of the time, Pallas kernels for 0%

profile of v1, /device:TPU:32, one launch (start us, length us, event | category | flops | bytes accessed | tf_op | source)
XLA Modules:
  0.0 413.6 jit_solution(17210579529651404349)
XLA Ops:
  6.5 0.9 multiply_add_fusion
  7.4 1.7 collective-permute-start
  9.2 1.3 collective-permute-start.1
  10.5 1.9 multiply_reduce_fusion.1
  12.4 0.6 convert_reduce_fusion
  13.0 2.2 collective-permute-done.1
  15.5 0.2 broadcast_select_fusion.19
  15.7 0.8 fusion.14
  16.4 37.9 %all-reduce.2 = (f32[256]{0:T(256)S(1)}, f32[]{:T(128)}, f32[]{:T(128)}) all-reduce(f32[256]{0:T(256)S(1)} %multiply_reduce_fusion.1, f32[]{:T(128)} %convert_reduce_fusion, f32[]{:T(128)} %fusion.14), channel_id=1, replica_groups=mesh['spot'=16,'gene'=16] {'spot'}, use_global_device_ids=true, to_apply=%region_1.2 | all-reduce | flops 258 | bytes 2064 | tf_op jit(solution)/shard_map/psum | solution.py:66
  54.3 0.6 broadcast_divide_fusion.1
  55.0 0.4 multiply_reduce_fusion
  55.4 19.0 %all-gather.1 = f32[16,1,256]{2,1,0:T(1,128)S(1)} all-gather(f32[1,1,256]{2,1,0:T(1,128)S(1)} %bitcast.7), channel_id=2, replica_groups=mesh['spot'=16,'gene'=16] {'spot'}, dimensions={0}, use_global_device_ids=true | all-gather | bytes 17408 | tf_op jit(solution)/shard_map/all_gather | solution.py:16
  74.4 0.7 add_sqrt_fusion
  75.1 0.4 divide_convert_fusion
  75.5 2.3 collective-permute-start.2
  77.8 1.3 collective-permute-start.3
  79.1 0.2 collective-permute-done.2
  79.3 5.1 %collective-permute-done.3 = bf16[2,512,256]{2,1,0:T(8,128)(2,1)S(1)} collective-permute-done((bf16[2,512,256]{2,1,0:T(8,128)(2,1)S(1)}, bf16[2,512,256]{2,1,0:T(8,128)(2,1)S(1)}, u32[]{:S(2)}, u32[]{:S(2)}) %collective-permute-start.3) | collective-permute-done | bytes 524320 | tf_op jit(solution)/shard_map/ppermute | solution.py:30
  84.4 0.7 fusion.5
  85.1 12.2 %add_convert_fusion = bf16[4,512,256]{2,1,0:T(8,128)(2,1)} fusion(bf16[4,512,256]{2,1,0:T(8,128)(2,1)S(1)} %divide_convert_fusion, bf16[2,512,256]{2,1,0:T(8,128)(2,1)S(1)} %collective-permute-done.3, bf16[2,512,256]{2,1,0:T(8,128)(2,1)S(1)} %collective-permute-done.2, bf16[8,516,256]{2,1,0:T(8,128)(2,1)S(1)} %fusion.5, f32[4,512]{1,0:T(4,128)S(1)} %get-tuple-element.92, ...), kind=kLoop, calls=%fused_computation.8 | loop fusion | flops 39845888 | bytes 24313856 | tf_op jit(solution)/shard_map/convert_element_type | solution.py:79
  97.4 211.2 %all-gather.4.cloned.1.call-done = bf16[2048,4096]{1,0:T(8,128)(2,1)} async-done(((bf16[2048,256]{1,0:T(8,128)(2,1)}), bf16[2048,4096]{1,0:T(8,128)(2,1)}) %all-gather.4.cloned.1.call-update) | async-done | bytes 16777232 | tf_op jit(solution)/shard_map/all_gather | solution.py:83
  308.6 10.1 %fusion.43 = f32[256,4096]{1,0:T(8,128)} fusion(bf16[2048,256]{1,0:T(8,128)(2,1)S(1)} %bitcast.5, bf16[2048,4096]{1,0:T(8,128)(2,1)} %all-gather.4.cloned.1.call-done), kind=kOutput, calls=%fused_computation.137 | convolution fusion | flops 4294967296 | bytes 22020096 | tf_op jit(solution)/shard_map/dot_general | solution.py:38
  319.4 85.7 %reduce-scatter.2.cloned.1.call-done = f32[256,256]{1,0:T(8,128)} async-done(((f32[256,4096]{1,0:T(8,128)}), f32[256,256]{1,0:T(8,128)}) %reduce-scatter.2.cloned.1.call-update) | async-done | bytes 262160 | tf_op jit(solution)/shard_map/reduce_scatter | solution.py:84
  405.1 1.7 broadcast_divide_fusion
  (18 shorter events, 0.5 us)
Async XLA Ops:
  6.5 8.8 %copy-start.1 = (s32[4,512]{1,0:T(4,128)S(1)}, s32[4,512]{1,0:T(4,128)}, u32[]{:S(2)}) copy-start(s32[4,512]{1,0:T(4,128)} %param.5) | copy-start | bytes 24580
  6.5 5.9 %copy-start.2 = (s32[4,512]{1,0:T(4,128)S(1)}, s32[4,512]{1,0:T(4,128)}, u32[]{:S(2)}) copy-start(s32[4,512]{1,0:T(4,128)} %param.4) | copy-start | bytes 24580
  6.5 48.5 %copy-start = (s32[4,512,256]{2,1,0:T(8,128)S(1)}, s32[4,512,256]{2,1,0:T(8,128)}, u32[]{:S(2)}) copy-start(s32[4,512,256]{2,1,0:T(8,128)} %param.3) | copy-start | bytes 6291460
  6.5 302.1 %all-gather.4.cloned.1.call-start = ((), (), s32[]{:S(2)}) async-start(), calls=%async_computation.1 | async-start | bytes 17825792 | tf_op jit(solution)/shard_map/all_gather | solution.py:83
  7.4 5.6 %collective-permute-start = (s32[2,512]{1,0:T(2,128)S(1)}, s32[2,512]{1,0:T(2,128)S(1)}, u32[]{:S(2)}, u32[]{:S(2)}) collective-permute-start(s32[2,512]{1,0:T(2,128)S(1)} %get-tuple-element.102), channel_id=1, source_target_pairs={{0,16},{16,32},{32,48},{48,64},{64,80},{80,96},{96,112},{112,128},... | collective-permute-start | bytes 12296 | tf_op jit(solution)/shard_map/ppermute | solution.py:28
  9.2 6.0 %collective-permute-start.1 = (s32[2,512]{1,0:T(2,128)S(1)}, s32[2,512]{1,0:T(2,128)S(1)}, u32[]{:S(2)}, u32[]{:S(2)}) collective-permute-start(s32[2,512]{1,0:T(2,128)S(1)} %get-tuple-element.103), channel_id=1, source_target_pairs={{16,0},{32,16},{48,32},{64,48},{80,64},{96,80},{112,96},{128,112},... | collective-permute-start | bytes 12296 | tf_op jit(solution)/shard_map/ppermute | solution.py:30
  75.5 3.8 collective-permute-start.2
  77.8 6.5 %collective-permute-start.3 = (bf16[2,512,256]{2,1,0:T(8,128)(2,1)S(1)}, bf16[2,512,256]{2,1,0:T(8,128)(2,1)S(1)}, u32[]{:S(2)}, u32[]{:S(2)}) collective-permute-start(bf16[2,512,256]{2,1,0:T(8,128)(2,1)S(1)} %get-tuple-element.57), channel_id=1, source_target_pairs={{16,0},{32,16},{48,32},{64,48},{80,64},{96,80},{112,96},{128,112},... | collective-permute-start | bytes 1572872 | tf_op jit(solution)/shard_map/ppermute | solution.py:30
  97.4 307.7 %reduce-scatter.2.cloned.1.call-start = ((), (), s32[]{:S(2)}) async-start(), calls=%async_computation.2 | async-start | bytes 4456448 | tf_op jit(solution)/shard_map/reduce_scatter | solution.py:84
Sparse Core Ops, SparseCore 0:
  97.5 211.0 all-gather.3
  318.9 86.1 reduce-scatter.1
